TPU v7x, 32 devices: a whole 2x2x4 slice. The times are simulated.
32 devices in a mesh: dp: 16 (over z, x, core), group: 2 (over y).
Axes of the slice: x: 2, y: 2, z: 4, core: 2. Of those that a mesh axis runs over, the one named last changes fastest.
Arguments:
- inputs: bfloat16 [32768, 2048], P('dp', 'group'), may hold values from -6 to 6
- grad_out: bfloat16 [32768, 2048], P(('dp', 'group')), may hold values from -0.0625 to 0.0625
- weight: bfloat16 [2048, 2048], P('group'), may hold values from -6 to 6
- old_basis: float32 [2048, 256], P('group'), may hold values from -0.125 to 0.125
- first_moment: float32 [256, 2048], P(None, 'dp'), may hold values from -6 to 6
- second_moment: float32 [256, 2048], P(None, 'dp'), may hold values from 0.1 to 3
Outputs:
- new_weight: bfloat16 [2048, 2048], P('group')
- new_first: float32 [256, 2048], P(None, 'dp')
- new_second: float32 [256, 2048], P(None, 'dp')
- new_basis: float32 [2048, 256], P('group')
All inputs are finite; a program needn't handle non-finite values.
Results may differ from a plain program's by a relative error of at most 0.011.
Values may be sent and summed in bfloat16 or wider, within the bound.
No kernel may reach another device: no remote copies, remote signals or barrier semaphores. Data moves between devices by JAX's collectives and lax.ppermute only.
A program may use at most 64 MiB of HBM per device.

v0:
```python
import jax
import jax.numpy as jnp
from jax import lax
from jax.sharding import PartitionSpec as P

NS_STEPS = 5
STEP = 10
BETA_ONE = 0.9
BETA_TWO = 0.99
ADAM_EPS = 1e-08
HIGHEST = lax.Precision.HIGHEST


def matmul(left, right):
    return jnp.dot(left, right, precision=HIGHEST)


def inner_gram(matrix):
    return lax.dot_general(matrix, matrix, (((0,), (0,)), ((), ())), precision=HIGHEST)


def refine_group(subspace):
    squares = lax.psum(jnp.sum(subspace * subspace), "group")
    iterate = subspace / jnp.sqrt(squares)
    for sweep in range(NS_STEPS):
        gram = lax.psum(inner_gram(iterate).astype(jnp.bfloat16), "group").astype(jnp.float32)
        iterate = 1.5 * iterate - 0.5 * matmul(iterate, gram)
    return iterate


def shards(inputs, grad_out, weight, old_basis, first_moment, second_moment):
    partial_grad = lax.dot_general(
        inputs,
        lax.all_gather(grad_out, "group", axis=0, tiled=True),
        (((0,), (0,)), ((), ())),
        preferred_element_type=jnp.float32,
    )
    grad_block = lax.psum_scatter(partial_grad, "dp", scatter_dimension=1, tiled=True)
    projected = lax.psum(matmul(old_basis.T, grad_block).astype(jnp.bfloat16), "group").astype(
        jnp.float32
    )
    new_first = BETA_ONE * first_moment + (1.0 - BETA_ONE) * projected
    new_second = BETA_TWO * second_moment + (1.0 - BETA_TWO) * projected * projected
    direction = (
        new_first
        / (1.0 - BETA_ONE**STEP)
        / (jnp.sqrt(new_second / (1.0 - BETA_TWO**STEP)) + ADAM_EPS)
    )
    col_count = grad_block.shape[1]
    col_offset = lax.axis_index("dp") * col_count
    own_cols = lax.dynamic_slice_in_dim(weight, col_offset, col_count, 1).astype(jnp.float32)
    updated = (own_cols - matmul(old_basis, direction)).astype(jnp.bfloat16)
    new_weight = lax.all_gather(updated, "dp", axis=1, tiled=True)
    subspace_terms = matmul(grad_block, projected.T)
    subspace = lax.psum(subspace_terms, "dp")
    new_basis = refine_group(subspace)
    return (new_weight, new_first, new_second, new_basis)


def solution(mesh):
    return jax.shard_map(
        shards,
        mesh=mesh,
        in_specs=(
            P("dp", "group"),
            P(("dp", "group"), None),
            P("group", None),
            P("group", None),
            P(None, "dp"),
            P(None, "dp"),
        ),
        out_specs=(P("group", None), P(None, "dp"), P(None, "dp"), P("group", None)),
        check_vma=False,
    )
```

profile of v0, /device:TPU:0, one launch (start us, length us, event | category | flops | bytes accessed | tf_op | source)
XLA Modules:
  0.0 558.3 jit_solution(406713574473706663)
XLA Ops:
  7.2 0.0 copy-start
  7.2 0.0 all-gather.3.cloned.1.call-start
  7.2 0.7 all-gather.3.cloned.1.call-update
  7.9 0.0 reduce-scatter.2.cloned.1.call-start
  8.0 108.3 %all-gather.3.cloned.1.call-done = bf16[2048,2048]{1,0:T(8,128)(2,1)} async-done(((bf16[1024,2048]{1,0:T(8,128)(2,1)}), bf16[2048,2048]{1,0:T(8,128)(2,1)}) %all-gather.3.cloned.1.call-update) | async-done | bytes 8388624 | tf_op jit(solution)/shard_map/all_gather | solution.py:34
  116.3 14.6 %fusion.21 = f32[1024,2048]{1,0:T(8,128)} fusion(bf16[2048,1024]{1,0:T(8,128)(2,1)} %param.6, bf16[2048,2048]{1,0:T(8,128)(2,1)} %all-gather.3.cloned.1.call-done), kind=kOutput, calls=%fused_computation.38 | convolution fusion | flops 8589934592 | bytes 20971520 | tf_op jit(solution)/shard_map/dot_general | solution.py:32
  130.9 0.0 reduce-scatter.2.cloned.1.call-update
  130.9 0.0 all-reduce.8.cloned.1.call-start
  130.9 103.7 %reduce-scatter.2.cloned.1.call-done = f32[1024,128]{1,0:T(8,128)} async-done(((f32[1024,2048]{1,0:T(8,128)}), f32[1024,128]{1,0:T(8,128)}) %reduce-scatter.2.cloned.1.call-update) | async-done | bytes 524304 | tf_op jit(solution)/shard_map/reduce_scatter | solution.py:38
  234.6 0.0 copy-done
  234.6 2.7 fusion.7
  237.4 0.0 all-reduce.8.cloned.1.call-update
  237.4 0.0 all-reduce.10.cloned.1.call-start
  237.4 20.7 %all-reduce.8.cloned.1.call-done = bf16[256,128]{0,1:T(8,128)(2,1)} async-done(((bf16[256,128]{0,1:T(8,128)(2,1)}), bf16[256,128]{0,1:T(8,128)(2,1)}) %all-reduce.8.cloned.1.call-update) | async-done | bytes 65552 | tf_op jit(solution)/shard_map/psum | solution.py:39
  258.1 2.6 fusion.22
  260.7 0.0 all-reduce.10.cloned.1.call-update
  260.7 0.0 all-reduce.12.cloned.1.call-start
  260.8 95.1 %all-reduce.10.cloned.1.call-done = f32[1024,256]{1,0:T(8,128)} async-done(((f32[1024,256]{1,0:T(8,128)}), f32[1024,256]{1,0:T(8,128)}) %all-reduce.10.cloned.1.call-update) | async-done | bytes 1048592 | tf_op jit(solution)/shard_map/psum | solution.py:55
  355.8 0.0 copy-start.1
  355.8 2.2 multiply_reduce_fusion
  358.0 5.5 psum.58
  364.3 4.0 convolution_convert_fusion.4
  368.3 0.0 all-reduce.12.cloned.1.call-update
  368.3 0.0 all-reduce.14.cloned.1.call-start
  368.4 20.7 %all-reduce.12.cloned.1.call-done = bf16[256,256]{1,0:T(8,128)(2,1)} async-done(((bf16[256,256]{1,0:T(8,128)(2,1)}), bf16[256,256]{1,0:T(8,128)(2,1)}) %all-reduce.12.cloned.1.call-update) | async-done | bytes 131088 | tf_op jit(solution)/shard_map/psum | solution.py:26
  389.1 0.0 copy-done.1
  389.1 1.6 fusion.4
  390.7 0.0 copy-start.2
  390.7 0.0 copy-start.3
  390.7 2.5 convolution_convert_fusion.3
  393.2 0.0 all-reduce.14.cloned.1.call-update
  393.2 0.2 all-reduce.16.cloned.1.call-start
  393.5 21.4 %all-reduce.14.cloned.1.call-done = bf16[256,256]{1,0:T(8,128)(2,1)} async-done(((bf16[256,256]{1,0:T(8,128)(2,1)}), bf16[256,256]{1,0:T(8,128)(2,1)}) %all-reduce.14.cloned.1.call-update) | async-done | bytes 131088 | tf_op jit(solution)/shard_map/psum | solution.py:26
  414.9 1.5 fusion.3
  416.4 2.5 convolution_convert_fusion.2
  418.9 0.0 all-reduce.16.cloned.1.call-update
  419.0 0.0 all-reduce.18.cloned.1.call-start
  419.0 1.0 constant_dynamic-slice_fusion
  420.0 0.9 copy.16
  420.8 0.0 copy-done.2
  420.8 0.1 copy.11
  420.9 0.0 copy-done.3
  421.0 0.8 copy.12
  421.7 18.9 %all-reduce.16.cloned.1.call-done = bf16[256,256]{1,0:T(8,128)(2,1)} async-done(((bf16[256,256]{1,0:T(8,128)(2,1)}), bf16[256,256]{1,0:T(8,128)(2,1)}) %all-reduce.16.cloned.1.call-update) | async-done | bytes 131088 | tf_op jit(solution)/shard_map/psum | solution.py:26
  440.6 1.5 fusion.2
  442.2 2.5 convolution_convert_fusion.1
  444.7 0.0 all-reduce.18.cloned.1.call-update
  444.7 0.0 all-reduce.20.cloned.1.call-start
  444.7 1.0 fusion.8
  445.7 20.6 %all-reduce.18.cloned.1.call-done = bf16[256,256]{1,0:T(8,128)(2,1)} async-done(((bf16[256,256]{1,0:T(8,128)(2,1)}), bf16[256,256]{1,0:T(8,128)(2,1)}) %all-reduce.18.cloned.1.call-update) | async-done | bytes 131088 | tf_op jit(solution)/shard_map/psum | solution.py:26
  466.4 1.5 fusion.1
  467.9 2.5 convolution_convert_fusion
  470.4 0.0 all-reduce.20.cloned.1.call-update
  470.4 0.0 all-gather.5.cloned.1.call-start
  470.5 2.9 fusion.6
  473.3 0.0 all-gather.5.cloned.1.call-update
  473.4 0.8 copy.14
  474.1 0.8 copy.15
  474.9 17.2 %all-reduce.20.cloned.1.call-done = bf16[256,256]{1,0:T(8,128)(2,1)} async-done(((bf16[256,256]{1,0:T(8,128)(2,1)}), bf16[256,256]{1,0:T(8,128)(2,1)}) %all-reduce.20.cloned.1.call-update) | async-done | bytes 131088 | tf_op jit(solution)/shard_map/psum | solution.py:26
  492.1 2.5 fusion
  494.6 50.5 %all-gather.5.cloned.1.call-done = bf16[1024,2048]{0,1:T(8,128)(2,1)} async-done(((bf16[1024,128]{0,1:T(8,128)(2,1)}), bf16[1024,2048]{0,1:T(8,128)(2,1)}) %all-gather.5.cloned.1.call-update) | async-done | bytes 4194320 | tf_op jit(solution)/shard_map/all_gather | solution.py:53
  545.1 6.4 %copy.13 = bf16[1024,2048]{1,0:T(8,128)(2,1)} copy(bf16[1024,2048]{0,1:T(8,128)(2,1)} %all-gather.5.cloned.1.call-done) | data formatting | bytes 8388608
Async XLA Ops:
  7.2 227.5 %copy-start = (f32[1024,256]{1,0:T(8,128)S(1)}, f32[1024,256]{1,0:T(8,128)}, u32[]{:S(2)}) copy-start(f32[1024,256]{1,0:T(8,128)} %param.9) | copy-start | bytes 3145732
  7.2 109.1 %all-gather.3.cloned.1.call-start = ((), (), s32[]{:S(2)}) async-start(), calls=%async_computation.1 | async-start | bytes 12582912 | tf_op jit(solution)/shard_map/all_gather | solution.py:34
  7.9 226.7 %reduce-scatter.2.cloned.1.call-start = ((), (), s32[]{:S(2)}) async-start(), calls=%async_computation.2 | async-start | bytes 8912896 | tf_op jit(solution)/shard_map/reduce_scatter | solution.py:38
  130.9 127.2 %all-reduce.8.cloned.1.call-start = ((), (), s32[]{:S(2)}) async-start(), calls=%async_computation.3 | async-start | bytes 131072 | tf_op jit(solution)/shard_map/psum | solution.py:39
  237.4 118.5 %all-reduce.10.cloned.1.call-start = ((), (), s32[]{:S(2)}) async-start(), calls=%async_computation.5 | async-start | bytes 2097152 | tf_op jit(solution)/shard_map/psum | solution.py:55
  260.7 128.4 %all-reduce.12.cloned.1.call-start = ((), (), s32[]{:S(2)}) async-start(), calls=%async_computation.6 | async-start | bytes 262144 | tf_op jit(solution)/shard_map/psum | solution.py:26
  355.8 33.3 %copy-start.1 = (f32[1024,256]{1,0:T(8,128)S(1)}, f32[1024,256]{1,0:T(8,128)}, u32[]{:S(2)}) copy-start(f32[1024,256]{1,0:T(8,128)} %all-reduce.10.cloned.1.call-done) | copy-start | bytes 3145732
  368.3 46.6 %all-reduce.14.cloned.1.call-start = ((), (), s32[]{:S(2)}) async-start(), calls=%async_computation.7 | async-start | bytes 262144 | tf_op jit(solution)/shard_map/psum | solution.py:26
  390.7 30.2 %copy-start.2 = (f32[256,128]{1,0:T(8,128)S(1)}, f32[256,128]{1,0:T(8,128)}, u32[]{:S(2)}) copy-start(f32[256,128]{1,0:T(8,128)} %param.10) | copy-start | bytes 393220
  390.7 30.3 %copy-start.3 = (f32[256,128]{1,0:T(8,128)S(1)}, f32[256,128]{1,0:T(8,128)}, u32[]{:S(2)}) copy-start(f32[256,128]{1,0:T(8,128)} %param.11) | copy-start | bytes 393220
  393.2 47.4 %all-reduce.16.cloned.1.call-start = ((), (), s32[]{:S(2)}) async-start(), calls=%async_computation.8 | async-start | bytes 262144 | tf_op jit(solution)/shard_map/psum | solution.py:26
  419.0 47.4 %all-reduce.18.cloned.1.call-start = ((), (), s32[]{:S(2)}) async-start(), calls=%async_computation.9 | async-start | bytes 262144 | tf_op jit(solution)/shard_map/psum | solution.py:26
  444.7 47.4 %all-reduce.20.cloned.1.call-start = ((), (), s32[]{:S(2)}) async-start(), calls=%async_computation.10 | async-start | bytes 262144 | tf_op jit(solution)/shard_map/psum | solution.py:26
  470.4 74.7 %all-gather.5.cloned.1.call-start = ((), (), s32[]{:S(2)}) async-start(), calls=%async_computation.4 | async-start | bytes 4456448 | tf_op jit(solution)/shard_map/all_gather | solution.py:53
Sparse Core Ops, SparseCore 0:
  9.5 106.6 all-gather.2
  131.0 103.5 reduce-scatter.1
  237.5 20.5 all-reduce.7
  262.0 93.7 all-reduce.9
  368.4 20.6 all-reduce.11
  393.4 21.5 all-reduce.13
  419.1 21.5 all-reduce.15
  444.8 21.5 all-reduce.17
  470.5 21.5 all-reduce.19
  494.7 50.3 all-gather.4
where the time goes:
time: 559 us; the launch traced here: 558 us
  waiting for transfers between devices  478 us (86%)
  matrix products  45.4 us (8%)
  between operations  15 us (3%)
  local copies, waits for them, and re-layouts  10.6 us (2%)
    all_gather x1, waiting for transfers between devices, shards(): lax.all_gather(grad_out, 'group', axis=0, tiled=True)  108 us
    reduce_scatter x1, waiting for transfers between devices, shards(): lax.psum_scatter(partial_grad, 'dp', scatter_dimension=1, tiled=True)  104 us
    psum x5, waiting for transfers between devices, refine_group(): lax.psum(inner_gram(iterate).astype(jnp.bfloat16), 'group')  99 us
    psum x1, waiting for transfers between devices, shards(): subspace = lax.psum(subspace_terms, 'dp')  95.1 us
    all_gather x1, waiting for transfers between devices, shards(): new_weight = lax.all_gather(updated, 'dp', axis=1, tiled=True)  50.5 us
    psum x1, waiting for transfers between devices, shards(): lax.psum(matmul(old_basis.T, grad_block).astype(jnp.bfloat16), 'group')  20.7 us
    dot_general x8, matrix products, matmul(): return jnp.dot(left, right, precision=HIGHEST)  16.8 us
    dot_general x1, matrix products, shards(): lax.dot_general(inputs, lax.all_gather(grad_out, 'group', axis=0, tiled=T...  14.6 us
  transfers between devices with their start and end apart: 10, of which 10 were waited for; matrix products, arithmetic and copies ran while one was open for 2% of the time, Pallas kernels for 0%

commit v1 on v0

--- a/solution.py
+++ b/solution.py
@@ -9,6 +9,10 @@
 BETA_TWO = 0.99
 ADAM_EPS = 1e-08
 HIGHEST = lax.Precision.HIGHEST
+
+
+def choose_lines(x0):
+    return jnp.sum(lax.all_gather(x0, "group"), axis=0)
 
 
 def matmul(left, right):
@@ -36,7 +40,7 @@
         preferred_element_type=jnp.float32,
     )
     grad_block = lax.psum_scatter(partial_grad, "dp", scatter_dimension=1, tiled=True)
-    projected = lax.psum(matmul(old_basis.T, grad_block).astype(jnp.bfloat16), "group").astype(
+    projected = choose_lines(matmul(old_basis.T, grad_block).astype(jnp.bfloat16)).astype(
         jnp.float32
     )
     new_first = BETA_ONE * first_moment + (1.0 - BETA_ONE) * projected

time: 559 us -> 541 us (0.968)
  waiting for transfers between devices: 478 us -> 455 us
    psum x1 -> x0, waiting for transfers between devices: 20.7 us -> none  [shards(): lax.psum(matmul(old_basis.T, grad_block).astype(jnp.bfloat16), 'group')]
  transfers between devices with their start and end apart: 10 -> 9, of which waited for: 10 -> 9; matrix products, arithmetic and copies ran while one was open for 2% -> 2% of each run, Pallas kernels for 0% -> 0%
where the time goes in v1:
time: 541 us
  waiting for transfers between devices  455 us (84%)
  matrix products  44.9 us (8%)
  between operations  14.6 us (3%)
  local copies, waits for them, and re-layouts  11.3 us (2%)
  blocking collectives  10.5 us (2%)
    all_gather x1, waiting for transfers between devices, shards(): lax.all_gather(grad_out, 'group', axis=0, tiled=True)  108 us
    reduce_scatter x1, waiting for transfers between devices, shards(): lax.psum_scatter(partial_grad, 'dp', scatter_dimension=1, tiled=True)  104 us
    psum x5, waiting for transfers between devices, refine_group(): lax.psum(inner_gram(iterate).astype(jnp.bfloat16), 'group')  98.3 us
    psum x1, waiting for transfers between devices, shards(): subspace = lax.psum(subspace_terms, 'dp')  93.4 us
    all_gather x1, waiting for transfers between devices, shards(): new_weight = lax.all_gather(updated, 'dp', axis=1, tiled=True)  50.6 us
    dot_general x8, matrix products, matmul(): return jnp.dot(left, right, precision=HIGHEST)  16.2 us
    dot_general x1, matrix products, shards(): lax.dot_general(inputs, lax.all_gather(grad_out, 'group', axis=0, tiled=T...  14.7 us
    dot_general x5, matrix products, inner_gram(): lax.dot_general(matrix, matrix, (((0,), (0,)), ((), ())), precision=HIGHEST)  14 us
  transfers between devices with their start and end apart: 9, of which 9 were waited for; matrix products, arithmetic and copies ran while one was open for 2% of the time, Pallas kernels for 0%

profile of v1, /device:TPU:0, one launch (start us, length us, event | category | flops | bytes accessed | tf_op | source)
XLA Modules:
  0.0 540.6 jit_solution(15344716914715569727)
XLA Ops:
  7.2 0.0 copy-start
  7.2 0.0 all-gather.4.cloned.1.call-start
  7.2 0.7 all-gather.4.cloned.1.call-update
  7.9 0.0 reduce-scatter.2.cloned.1.call-start
  8.0 108.3 %all-gather.4.cloned.1.call-done = bf16[2048,2048]{1,0:T(8,128)(2,1)} async-done(((bf16[1024,2048]{1,0:T(8,128)(2,1)}), bf16[2048,2048]{1,0:T(8,128)(2,1)}) %all-gather.4.cloned.1.call-update) | async-done | bytes 8388624 | tf_op jit(solution)/shard_map/all_gather | solution.py:38
  116.3 14.7 %fusion.21 = f32[1024,2048]{1,0:T(8,128)} fusion(bf16[2048,1024]{1,0:T(8,128)(2,1)} %param.6, bf16[2048,2048]{1,0:T(8,128)(2,1)} %all-gather.4.cloned.1.call-done), kind=kOutput, calls=%fused_computation.38 | convolution fusion | flops 8589934592 | bytes 20971520 | tf_op jit(solution)/shard_map/dot_general | solution.py:36
  131.0 0.0 reduce-scatter.2.cloned.1.call-update
  131.0 0.0 all-reduce.7.cloned.1.call-start
  131.1 103.7 %reduce-scatter.2.cloned.1.call-done = f32[1024,128]{1,0:T(8,128)} async-done(((f32[1024,2048]{1,0:T(8,128)}), f32[1024,128]{1,0:T(8,128)}) %reduce-scatter.2.cloned.1.call-update) | async-done | bytes 524304 | tf_op jit(solution)/shard_map/reduce_scatter | solution.py:42
  234.8 0.0 copy-done
  234.8 2.1 fusion.7
  236.8 4.9 all-gather
  241.8 0.3 reduce_sum.21
  242.1 2.6 fusion.22
  244.7 0.0 all-reduce.7.cloned.1.call-update
  244.8 0.0 all-reduce.9.cloned.1.call-start
  244.8 93.4 %all-reduce.7.cloned.1.call-done = f32[1024,256]{1,0:T(8,128)} async-done(((f32[1024,256]{1,0:T(8,128)}), f32[1024,256]{1,0:T(8,128)}) %all-reduce.7.cloned.1.call-update) | async-done | bytes 1048592 | tf_op jit(solution)/shard_map/psum | solution.py:59
  338.2 0.0 copy-start.1
  338.2 2.2 multiply_reduce_fusion
  340.4 5.5 %psum.50 = f32[]{:T(128)} all-reduce(f32[]{:T(128)} %multiply_reduce_fusion), channel_id=1, replica_groups=mesh['dp'=16,'group'=2] {'group'}, use_global_device_ids=true, to_apply=%region_4.0 | all-reduce | flops 1 | bytes 8 | tf_op jit(solution)/shard_map/psum | solution.py:27
  346.6 4.0 convolution_convert_fusion.4
  350.7 0.0 all-reduce.9.cloned.1.call-update
  350.7 0.0 all-reduce.11.cloned.1.call-start
  350.8 20.7 %all-reduce.9.cloned.1.call-done = bf16[256,256]{1,0:T(8,128)(2,1)} async-done(((bf16[256,256]{1,0:T(8,128)(2,1)}), bf16[256,256]{1,0:T(8,128)(2,1)}) %all-reduce.9.cloned.1.call-update) | async-done | bytes 131088 | tf_op jit(solution)/shard_map/psum | solution.py:30
  371.5 0.0 copy-done.1
  371.5 1.6 fusion.4
  373.1 0.0 copy-start.2
  373.1 0.0 copy-start.3
  373.1 2.5 convolution_convert_fusion.3
  375.6 0.0 all-reduce.11.cloned.1.call-update
  375.6 0.2 all-reduce.13.cloned.1.call-start
  375.8 21.4 %all-reduce.11.cloned.1.call-done = bf16[256,256]{1,0:T(8,128)(2,1)} async-done(((bf16[256,256]{1,0:T(8,128)(2,1)}), bf16[256,256]{1,0:T(8,128)(2,1)}) %all-reduce.11.cloned.1.call-update) | async-done | bytes 131088 | tf_op jit(solution)/shard_map/psum | solution.py:30
  397.3 1.5 fusion.3
  398.8 2.5 convolution_convert_fusion.2
  401.3 0.0 all-reduce.13.cloned.1.call-update
  401.3 0.0 all-reduce.15.cloned.1.call-start
  401.4 1.0 constant_dynamic-slice_fusion
  402.4 0.9 copy.18
  403.2 0.0 copy-done.2
  403.2 0.8 copy.13
  404.0 0.0 copy-done.3
  404.0 0.8 copy.14
  404.7 18.3 %all-reduce.13.cloned.1.call-done = bf16[256,256]{1,0:T(8,128)(2,1)} async-done(((bf16[256,256]{1,0:T(8,128)(2,1)}), bf16[256,256]{1,0:T(8,128)(2,1)}) %all-reduce.13.cloned.1.call-update) | async-done | bytes 131088 | tf_op jit(solution)/shard_map/psum | solution.py:30
  423.0 1.5 fusion.2
  424.5 2.5 convolution_convert_fusion.1
  427.0 0.0 all-reduce.15.cloned.1.call-update
  427.1 0.0 all-reduce.17.cloned.1.call-start
  427.1 1.0 fusion.8
  428.1 20.6 %all-reduce.15.cloned.1.call-done = bf16[256,256]{1,0:T(8,128)(2,1)} async-done(((bf16[256,256]{1,0:T(8,128)(2,1)}), bf16[256,256]{1,0:T(8,128)(2,1)}) %all-reduce.15.cloned.1.call-update) | async-done | bytes 131088 | tf_op jit(solution)/shard_map/psum | solution.py:30
  448.7 1.5 fusion.1
  450.3 2.5 convolution_convert_fusion
  452.8 0.0 all-reduce.17.cloned.1.call-update
  452.8 0.0 all-gather.6.cloned.1.call-start
  452.8 2.9 fusion.6
  455.7 0.0 all-gather.6.cloned.1.call-update
  455.7 0.8 copy.16
  456.5 0.8 copy.17
  457.3 17.2 %all-reduce.17.cloned.1.call-done = bf16[256,256]{1,0:T(8,128)(2,1)} async-done(((bf16[256,256]{1,0:T(8,128)(2,1)}), bf16[256,256]{1,0:T(8,128)(2,1)}) %all-reduce.17.cloned.1.call-update) | async-done | bytes 131088 | tf_op jit(solution)/shard_map/psum | solution.py:30
  474.5 2.5 fusion
  477.0 50.6 %all-gather.6.cloned.1.call-done = bf16[1024,2048]{0,1:T(8,128)(2,1)} async-done(((bf16[1024,128]{0,1:T(8,128)(2,1)}), bf16[1024,2048]{0,1:T(8,128)(2,1)}) %all-gather.6.cloned.1.call-update) | async-done | bytes 4194320 | tf_op jit(solution)/shard_map/all_gather | solution.py:57
  527.6 6.4 %copy.15 = bf16[1024,2048]{1,0:T(8,128)(2,1)} copy(bf16[1024,2048]{0,1:T(8,128)(2,1)} %all-gather.6.cloned.1.call-done) | data formatting | bytes 8388608
  (1 shorter events, 0.0 us)
Async XLA Ops:
  7.2 227.6 %copy-start = (f32[1024,256]{1,0:T(8,128)S(1)}, f32[1024,256]{1,0:T(8,128)}, u32[]{:S(2)}) copy-start(f32[1024,256]{1,0:T(8,128)} %param.9) | copy-start | bytes 3145732
  7.2 109.1 %all-gather.4.cloned.1.call-start = ((), (), s32[]{:S(2)}) async-start(), calls=%async_computation.1 | async-start | bytes 12582912 | tf_op jit(solution)/shard_map/all_gather | solution.py:38
  7.9 226.8 %reduce-scatter.2.cloned.1.call-start = ((), (), s32[]{:S(2)}) async-start(), calls=%async_computation.2 | async-start | bytes 8912896 | tf_op jit(solution)/shard_map/reduce_scatter | solution.py:42
  131.0 207.2 %all-reduce.7.cloned.1.call-start = ((), (), s32[]{:S(2)}) async-start(), calls=%async_computation.4 | async-start | bytes 2097152 | tf_op jit(solution)/shard_map/psum | solution.py:59
  244.8 126.7 %all-reduce.9.cloned.1.call-start = ((), (), s32[]{:S(2)}) async-start(), calls=%async_computation.5 | async-start | bytes 262144 | tf_op jit(solution)/shard_map/psum | solution.py:30
  338.2 33.3 %copy-start.1 = (f32[1024,256]{1,0:T(8,128)S(1)}, f32[1024,256]{1,0:T(8,128)}, u32[]{:S(2)}) copy-start(f32[1024,256]{1,0:T(8,128)} %all-reduce.7.cloned.1.call-done) | copy-start | bytes 3145732
  350.7 46.6 %all-reduce.11.cloned.1.call-start = ((), (), s32[]{:S(2)}) async-start(), calls=%async_computation.6 | async-start | bytes 262144 | tf_op jit(solution)/shard_map/psum | solution.py:30
  373.1 30.2 %copy-start.2 = (f32[256,128]{1,0:T(8,128)S(1)}, f32[256,128]{1,0:T(8,128)}, u32[]{:S(2)}) copy-start(f32[256,128]{1,0:T(8,128)} %param.10) | copy-start | bytes 393220
  373.1 30.9 %copy-start.3 = (f32[256,128]{1,0:T(8,128)S(1)}, f32[256,128]{1,0:T(8,128)}, u32[]{:S(2)}) copy-start(f32[256,128]{1,0:T(8,128)} %param.11) | copy-start | bytes 393220
  375.6 47.4 %all-reduce.13.cloned.1.call-start = ((), (), s32[]{:S(2)}) async-start(), calls=%async_computation.7 | async-start | bytes 262144 | tf_op jit(solution)/shard_map/psum | solution.py:30
  401.3 47.4 %all-reduce.15.cloned.1.call-start = ((), (), s32[]{:S(2)}) async-start(), calls=%async_computation.8 | async-start | bytes 262144 | tf_op jit(solution)/shard_map/psum | solution.py:30
  427.1 47.4 %all-reduce.17.cloned.1.call-start = ((), (), s32[]{:S(2)}) async-start(), calls=%async_computation.9 | async-start | bytes 262144 | tf_op jit(solution)/shard_map/psum | solution.py:30
  452.8 74.8 %all-gather.6.cloned.1.call-start = ((), (), s32[]{:S(2)}) async-start(), calls=%async_computation.3 | async-start | bytes 4456448 | tf_op jit(solution)/shard_map/all_gather | solution.py:57
Sparse Core Ops, SparseCore 0:
  9.5 106.6 all-gather.3
  131.1 103.5 reduce-scatter.1
  244.9 93.2 all-reduce.6
  350.8 20.6 all-reduce.8
  375.7 21.5 all-reduce.10
  401.5 21.5 all-reduce.12
  427.2 21.5 all-reduce.14
  452.9 21.5 all-reduce.16
  477.2 50.3 all-gather.5
